TPU v7x, 512 devices: a whole 4x8x8 slice. The times are simulated.
512 devices in a mesh: dp: 16 (over x, y_hi, core), tensor: 32 (over y_lo, z).
Axes of the slice: x: 4, y: 8 (y_hi: 2, y_lo: 4; y = y_hi * 4 + y_lo), z: 8, core: 2. Of those that a mesh axis runs over, the one named last changes fastest.
Arguments:
- tokens: bfloat16 [8192, 8192], P('dp', 'tensor'), may hold values from -6 to 6
- first_right: bfloat16 [32, 256, 1024], P('tensor'), may hold values from -0.375 to 0.375
- first_left: bfloat16 [128, 256, 256], P('tensor'), may hold values from -0.375 to 0.375
- second_right: bfloat16 [128, 256, 256], P('tensor'), may hold values from -0.375 to 0.375
- second_left: bfloat16 [32, 1024, 256], P('tensor'), may hold values from -0.1875 to 0.1875
- cotangent: bfloat16 [8192, 8192], P('dp', 'tensor'), may hold values from -6 to 6
Outputs:
- layer_out: bfloat16 [8192, 8192], P('dp', 'tensor')
- grad_tokens: bfloat16 [8192, 8192], P('dp', 'tensor')
- grad_first_right: float32 [32, 256, 1024], P('tensor', 'dp')
- grad_first_left: float32 [128, 256, 256], P('tensor', 'dp')
- grad_second_right: float32 [128, 256, 256], P('tensor', 'dp')
- grad_second_left: float32 [32, 1024, 256], P('tensor', 'dp')
All inputs are finite; a program needn't handle non-finite values.
Results may differ from a plain program's by a relative error of at most 0.018.
Values may be sent and summed in bfloat16 or wider, within the bound.
No kernel may reach another device: no remote copies, remote signals or barrier semaphores. Data moves between devices by JAX's collectives and lax.ppermute only.
A program may use at most 64 MiB of HBM per device.

v0:
```python
import jax
import jax.numpy as jnp
from jax import lax
from jax.sharding import PartitionSpec as P

half_root = 0.7071067811865476
inv_root_two_pi = 0.3989422804014327


def gelu_value(value):
    return 0.5 * value * (1.0 + jax.scipy.special.erf(value * half_root))


def gelu_slope(value):
    return (
        0.5 * (1.0 + jax.scipy.special.erf(value * half_root))
        + value * jnp.exp(-0.5 * value * value) * inv_root_two_pi
    )


def shards(tokens, first_right, first_left, second_right, second_left, cotangent):
    fp = jnp.float32
    bf = jnp.bfloat16
    tok_rows = tokens.shape[0]
    in_blocks = first_right.shape[0]
    block_width = first_right.shape[1]
    wide_width = first_right.shape[2]
    hid_blocks = first_left.shape[0]
    groups = lax.axis_size("tensor")
    replicas = lax.axis_size("dp")
    all_in = in_blocks * groups
    all_hid = hid_blocks * groups
    sub_width = wide_width // all_hid
    grad_scale = float(tok_rows * replicas) ** (-0.5)
    right_one = first_right.reshape(in_blocks, block_width, all_hid, sub_width)
    right_two = second_right.reshape(hid_blocks, block_width, all_in, sub_width)
    tok_parts = tokens.reshape(tok_rows, in_blocks, block_width)
    cot_parts = cotangent.reshape(tok_rows, in_blocks, block_width)
    up_inner = jnp.einsum("tkb,kbjg->jkgt", tok_parts, right_one, preferred_element_type=fp).astype(
        bf
    )
    arrived = lax.all_to_all(up_inner, "tensor", split_axis=0, concat_axis=1, tiled=True)
    mixed_piece = arrived.reshape(hid_blocks, block_width, arrived.shape[3])
    pre_piece = jnp.einsum("jbt,jbc->jct", mixed_piece, first_left, preferred_element_type=fp)
    hidden = gelu_value(pre_piece).astype(bf)
    down_inner = jnp.einsum("jbt,jbkg->kjgt", hidden, right_two, preferred_element_type=fp).astype(
        bf
    )
    mixed_down = lax.all_to_all(down_inner, "tensor", split_axis=0, concat_axis=1, tiled=True)
    mixed_down = mixed_down.reshape(in_blocks, wide_width, tok_rows)
    layer_out = jnp.einsum(
        "kwt,kwc->tkc", mixed_down, second_left, preferred_element_type=fp
    ).astype(bf)
    layer_out = layer_out.reshape(tok_rows, in_blocks * block_width)
    reduced = {}
    d_mixed_down = jnp.einsum(
        "tkc,kwc->kwt", cot_parts, second_left, preferred_element_type=fp
    ).astype(bf)
    d_mixed_down = d_mixed_down.reshape(in_blocks, all_hid, sub_width, tok_rows)
    d_down_inner = lax.all_to_all(d_mixed_down, "tensor", split_axis=1, concat_axis=0, tiled=True)
    d_hidden = jnp.einsum("kjgt,jbkg->jbt", d_down_inner, right_two, preferred_element_type=fp)
    d_pre = (d_hidden * gelu_slope(pre_piece)).astype(bf)
    d_mixed_up = jnp.einsum("jct,jbc->jbt", d_pre, first_left, preferred_element_type=fp).astype(bf)
    d_mixed_up = d_mixed_up.reshape(hid_blocks, all_in, sub_width, tok_rows)
    d_up_inner = lax.all_to_all(d_mixed_up, "tensor", split_axis=1, concat_axis=0, tiled=True)
    grad_tokens = jnp.einsum(
        "jkgt,kbjg->tkb", d_up_inner, right_one, preferred_element_type=fp
    ).astype(bf)
    grad_tokens = grad_tokens.reshape(tok_rows, in_blocks * block_width)
    result = jnp.einsum("jbt,kjgt->bjkg", hidden, d_down_inner, preferred_element_type=fp)
    term_result = jnp.einsum("tkb,jkgt->bkjg", tok_parts, d_up_inner, preferred_element_type=fp)
    summed = (
        lax.psum_scatter(
            (term_result.reshape(block_width, in_blocks, wide_width) * grad_scale).astype(
                jnp.bfloat16
            ),
            "dp",
            scatter_dimension=0,
            tiled=True,
        ).astype(jnp.float32),
        lax.psum_scatter(
            (
                jnp.einsum("jbt,jct->bjc", mixed_piece, d_pre, preferred_element_type=fp)
                * grad_scale
            ).astype(jnp.bfloat16),
            "dp",
            scatter_dimension=0,
            tiled=True,
        ).astype(jnp.float32),
        lax.psum_scatter(
            (result.reshape(block_width, hid_blocks, block_width) * grad_scale).astype(
                jnp.bfloat16
            ),
            "dp",
            scatter_dimension=0,
            tiled=True,
        ).astype(jnp.float32),
        lax.psum_scatter(
            (
                jnp.einsum("kwt,tkc->wkc", mixed_down, cot_parts, preferred_element_type=fp)
                * grad_scale
            ).astype(jnp.bfloat16),
            "dp",
            scatter_dimension=0,
            tiled=True,
        ).astype(jnp.float32),
    )
    reduced["right_one"] = summed[0]
    reduced["left_one"] = summed[1]
    reduced["right_two"] = summed[2]
    reduced["left_two"] = summed[3]
    grad_right_one = jnp.transpose(reduced["right_one"], (1, 0, 2))
    grad_left_one = jnp.transpose(reduced["left_one"], (1, 0, 2))
    grad_right_two = jnp.transpose(reduced["right_two"], (1, 0, 2))
    grad_left_two = jnp.transpose(reduced["left_two"], (1, 0, 2))
    return (layer_out, grad_tokens, grad_right_one, grad_left_one, grad_right_two, grad_left_two)


def solution(mesh):
    in_specs = (
        P("dp", "tensor"),
        P("tensor", None, None),
        P("tensor", None, None),
        P("tensor", None, None),
        P("tensor", None, None),
        P("dp", "tensor"),
    )
    out_specs = (
        P("dp", "tensor"),
        P("dp", "tensor"),
        P("tensor", "dp", None),
        P("tensor", "dp", None),
        P("tensor", "dp", None),
        P("tensor", "dp", None),
    )
    return jax.shard_map(shards, mesh=mesh, in_specs=in_specs, out_specs=out_specs, check_vma=False)
```

profile of v0, /device:TPU:1, one launch (start us, length us, event | category | flops | bytes accessed | tf_op | source)
XLA Modules:
  0.0 503.9 jit_solution(12077980124356621023)
XLA Ops:
  7.2 0.0 copy-start
  7.2 1.3 copy.71
  8.5 1.4 fusion.10
  9.9 1.6 copy.73
  11.5 14.3 %all-to-all-start = ((bf16[128,1,8,512]{3,2,1,0:T(8,128)(2,1)}), bf16[128,1,8,512]{3,2,1,0:T(8,128)(2,1)S(1)}, u32[]{:S(2)}, u32[]{:S(2)}) async-start(bf16[128,1,8,512]{3,2,1,0:T(8,128)(2,1)} %copy.73), calls=%async_computation | async-start | bytes 2097152 | tf_op jit(solution)/shard_map/all_to_all | solution.py:42
  25.8 1.5 fusion.11
  27.3 24.4 %all-to-all-done = bf16[128,1,8,512]{3,2,1,0:T(8,128)(2,1)S(1)} async-done(((bf16[128,1,8,512]{3,2,1,0:T(8,128)(2,1)}), bf16[128,1,8,512]{3,2,1,0:T(8,128)(2,1)S(1)}, u32[]{:S(2)}, u32[]{:S(2)}) %all-to-all-start) | async-done | bytes 1048608 | tf_op jit(solution)/shard_map/all_to_all | solution.py:42
  51.6 7.6 %all-to-all-start.2 = ((bf16[1,128,8,512]{3,2,0,1:T(8,128)(2,1)}), bf16[1,128,8,512]{3,2,0,1:T(8,128)(2,1)S(1)}, u32[]{:S(2)}, u32[]{:S(2)}) async-start(bf16[1,128,8,512]{3,2,0,1:T(8,128)(2,1)} %fusion.11), calls=%async_computation.2 | async-start | bytes 2097152 | tf_op jit(solution)/shard_map/all_to_all | solution.py:60
  59.2 2.0 copy.76
  61.3 0.5 fusion.25
  61.8 1.3 copy-done.1
  63.1 0.7 fusion.12
  63.9 1.5 copy.79
  65.4 19.5 %all-to-all-done.2 = bf16[1,128,8,512]{3,2,0,1:T(8,128)(2,1)S(1)} async-done(((bf16[1,128,8,512]{3,2,0,1:T(8,128)(2,1)}), bf16[1,128,8,512]{3,2,0,1:T(8,128)(2,1)S(1)}, u32[]{:S(2)}, u32[]{:S(2)}) %all-to-all-start.2) | async-done | bytes 1048608 | tf_op jit(solution)/shard_map/all_to_all | solution.py:60
  84.9 1.0 copy-done.3
  85.9 7.7 %all-to-all-start.1 = ((bf16[32,4,8,512]{3,2,1,0:T(8,128)(2,1)}), bf16[32,4,8,512]{3,2,1,0:T(8,128)(2,1)S(1)}, u32[]{:S(2)}, u32[]{:S(2)}) async-start(bf16[32,4,8,512]{3,2,1,0:T(8,128)(2,1)} %copy.79), calls=%async_computation.1 | async-start | bytes 2097152 | tf_op jit(solution)/shard_map/all_to_all | solution.py:49
  93.7 3.2 fusion.5
  96.9 0.5 fusion.13
  97.4 0.5 copy-done.2
  97.9 1.1 copy.83
  99.0 20.4 %all-to-all-done.1 = bf16[32,4,8,512]{3,2,1,0:T(8,128)(2,1)S(1)} async-done(((bf16[32,4,8,512]{3,2,1,0:T(8,128)(2,1)}), bf16[32,4,8,512]{3,2,1,0:T(8,128)(2,1)S(1)}, u32[]{:S(2)}, u32[]{:S(2)}) %all-to-all-start.1) | async-done | bytes 1048608 | tf_op jit(solution)/shard_map/all_to_all | solution.py:49
  119.4 7.9 %all-to-all-start.3 = ((bf16[4,32,8,512]{3,2,0,1:T(8,128)(2,1)}), bf16[4,32,8,512]{3,2,0,1:T(8,128)(2,1)}, u32[]{:S(2)}, u32[]{:S(2)}) async-start(bf16[4,32,8,512]{3,2,0,1:T(8,128)(2,1)} %copy.83), calls=%async_computation.3 | async-start | bytes 2097152 | tf_op jit(solution)/shard_map/all_to_all | solution.py:65
  127.2 0.0 reduce-scatter.3.cloned.1.call-start
  127.3 3.4 fusion.20
  130.7 2.0 copy.91
  132.7 0.0 reduce-scatter.3.cloned.1.call-update
  132.7 0.0 reduce-scatter.5.cloned.1.call-start
  132.8 1.3 dynamic-slice
  134.7 1.3 fusion.18
  136.0 0.0 reduce-scatter.5.cloned.1.call-update
  136.0 0.0 all-reduce.5.cloned.1.call-start
  136.1 2.6 fusion.21
  138.6 2.1 copy.88
  140.7 74.1 %reduce-scatter.3.cloned.1.call-done = bf16[16,4,256]{2,0,1:T(8,128)(2,1)} async-done(((bf16[256,4,256]{2,0,1:T(8,128)(2,1)}), bf16[16,4,256]{2,0,1:T(8,128)(2,1)}) %reduce-scatter.3.cloned.1.call-update) | async-done | bytes 32784 | tf_op jit(solution)/shard_map/reduce_scatter | solution.py:90
  214.8 1.4 convert_bitcast_fusion
  216.2 2.0 fusion.19
  218.3 0.3 copy.122
  218.6 2.1 copy.86
  220.7 1.2 convolution_convert_fusion.4
  221.9 0.0 all-reduce.5.cloned.1.call-update
  221.9 2.5 fusion.22
  224.3 76.8 %reduce-scatter.5.cloned.1.call-done = bf16[64,1,256]{2,0,1:T(8,128)(2,1)} async-done(((bf16[1024,1,256]{2,0,1:T(8,128)(2,1)}), bf16[64,1,256]{2,0,1:T(8,128)(2,1)}) %reduce-scatter.5.cloned.1.call-update) | async-done | bytes 32784 | tf_op jit(solution)/shard_map/reduce_scatter | solution.py:98
  301.1 1.4 bitcast_convert_fusion.1
  302.5 191.9 %all-reduce.5.cloned.1.call-done = (bf16[256,1,1024]{2,1,0:T(2,128)(2,1)}, bf16[256,4,256]{2,1,0:T(4,128)(2,1)}) async-done(((bf16[256,1,1024]{2,1,0:T(2,128)(2,1)}, bf16[256,4,256]{2,1,0:T(4,128)(2,1)}), (bf16[256,1,1024]{2,1,0:T(2,128)(2,1)}, bf16[256,4,256]{2,1,0:T(4,128)(2,1)})) %all-reduce.5.cloned.1.call-update) | async-done | bytes 1048592
  494.4 0.9 bitcast_convert_fusion
  495.3 0.8 convert_bitcast_fusion.1
  496.1 0.6 copy.93
  496.7 0.6 copy.92
  (15 shorter events, 0.0 us)
Async XLA Ops:
  7.2 54.1 %copy-start = (bf16[4,256,256]{2,1,0:T(8,128)(2,1)S(1)}, bf16[4,256,256]{2,1,0:T(8,128)(2,1)}, u32[]{:S(2)}) copy-start(bf16[4,256,256]{2,1,0:T(8,128)(2,1)} %param.8) | copy-start | bytes 1572868
  9.9 15.9 %copy-start.4 = (bf16[1,1024,256]{2,1,0:T(8,128)(2,1)S(1)}, bf16[1,1024,256]{2,1,0:T(8,128)(2,1)}, u32[]{:S(2)}) copy-start(bf16[1,1024,256]{2,1,0:T(8,128)(2,1)} %param.10) | copy-start | bytes 1572868
  9.9 15.9 %copy-start.7 = (bf16[512,256]{1,0:T(8,128)(2,1)S(1)}, bf16[512,256]{1,0:T(8,128)(2,1)}, u32[]{:S(2)}) copy-start(bf16[512,256]{1,0:T(8,128)(2,1)} %param.11) | copy-start | bytes 786436
  11.5 40.1 %all-to-all-start = ((bf16[128,1,8,512]{3,2,1,0:T(8,128)(2,1)}), bf16[128,1,8,512]{3,2,1,0:T(8,128)(2,1)S(1)}, u32[]{:S(2)}, u32[]{:S(2)}) async-start(bf16[128,1,8,512]{3,2,1,0:T(8,128)(2,1)} %copy.73), calls=%async_computation | async-start | bytes 2097152 | tf_op jit(solution)/shard_map/all_to_all | solution.py:42
  51.6 33.3 %all-to-all-start.2 = ((bf16[1,128,8,512]{3,2,0,1:T(8,128)(2,1)}), bf16[1,128,8,512]{3,2,0,1:T(8,128)(2,1)S(1)}, u32[]{:S(2)}, u32[]{:S(2)}) async-start(bf16[1,128,8,512]{3,2,0,1:T(8,128)(2,1)} %fusion.11), calls=%async_computation.2 | async-start | bytes 2097152 | tf_op jit(solution)/shard_map/all_to_all | solution.py:60
  61.3 1.9 copy-start.6
  61.8 1.3 copy-start.1
  84.9 1.0 copy-start.3
  85.9 33.4 %all-to-all-start.1 = ((bf16[32,4,8,512]{3,2,1,0:T(8,128)(2,1)}), bf16[32,4,8,512]{3,2,1,0:T(8,128)(2,1)S(1)}, u32[]{:S(2)}, u32[]{:S(2)}) async-start(bf16[32,4,8,512]{3,2,1,0:T(8,128)(2,1)} %copy.79), calls=%async_computation.1 | async-start | bytes 2097152 | tf_op jit(solution)/shard_map/all_to_all | solution.py:49
  96.9 1.0 copy-start.2
  119.4 96.8 %all-to-all-start.3 = ((bf16[4,32,8,512]{3,2,0,1:T(8,128)(2,1)}), bf16[4,32,8,512]{3,2,0,1:T(8,128)(2,1)}, u32[]{:S(2)}, u32[]{:S(2)}) async-start(bf16[4,32,8,512]{3,2,0,1:T(8,128)(2,1)} %copy.83), calls=%async_computation.3 | async-start | bytes 2097152 | tf_op jit(solution)/shard_map/all_to_all | solution.py:65
  127.2 87.6 %reduce-scatter.3.cloned.1.call-start = ((), (), s32[]{:S(2)}) async-start(), calls=%async_computation.6 | async-start | bytes 557056 | tf_op jit(solution)/shard_map/reduce_scatter | solution.py:90
  132.7 168.4 %reduce-scatter.5.cloned.1.call-start = ((), (), s32[]{:S(2)}) async-start(), calls=%async_computation.7 | async-start | bytes 557056 | tf_op jit(solution)/shard_map/reduce_scatter | solution.py:98
  136.0 80.2 %copy-start.8 = (bf16[512,256]{1,0:T(8,128)(2,1)S(1)}, bf16[512,256]{1,0:T(8,128)(2,1)}, u32[]{:S(2)}) copy-start(bf16[512,256]{1,0:T(8,128)(2,1)} %param.6) | copy-start | bytes 786436
  136.0 358.4 %all-reduce.5.cloned.1.call-start = ((), (), s32[]{:S(2)}) async-start(), calls=%async_computation.8 | async-start | bytes 3145728
  216.2 4.5 copy-start.5
Sparse Core Ops, SparseCore 0:
  132.9 81.9 reduce-scatter.2
  219.4 81.6 reduce-scatter.4
  304.1 190.2 all-reduce.4
where the time goes:
time: 505 us; the launch traced here: 504 us
  waiting for transfers between devices  407 us (81%)
  starting transfers between devices  37.6 us (7%)
  matrix products  20.7 us (4%)
  local copies, waits for them, and re-layouts  19.5 us (4%)
  between operations  14.6 us (3%)
    unnamed x4, waiting for transfers between devices  192 us
    reduce_scatter x1, waiting for transfers between devices, shards(): lax.psum_scatter((jnp.einsum('kwt,tkc->wkc', mixed_down, cot_parts, prefe...  76.8 us
    reduce_scatter x1, waiting for transfers between devices, shards(): lax.psum_scatter((result.reshape(block_width, hid_blocks, block_width) *...  74.1 us
    all_to_all x1, waiting for transfers between devices, shards(): lax.all_to_all(up_inner, 'tensor', split_axis=0, concat_axis=1, tiled=True)  24.4 us
    all_to_all x1, waiting for transfers between devices, shards(): lax.all_to_all(down_inner, 'tensor', split_axis=0, concat_axis=1, tiled=T...  20.4 us
    all_to_all x1, waiting for transfers between devices, shards(): lax.all_to_all(d_mixed_down, 'tensor', split_axis=1, concat_axis=0, tiled...  19.5 us
    all_to_all x1, starting transfers between devices, shards(): lax.all_to_all(up_inner, 'tensor', split_axis=0, concat_axis=1, tiled=True)  14.3 us
  transfers between devices with their start and end apart: 7, of which 6 were waited for; matrix products, arithmetic and copies ran while one was open for 7% of the time, Pallas kernels for 0%

commit v1 on v0

--- a/solution.py
+++ b/solution.py
@@ -39,7 +39,12 @@
     up_inner = jnp.einsum("tkb,kbjg->jkgt", tok_parts, right_one, preferred_element_type=fp).astype(
         bf
     )
-    arrived = lax.all_to_all(up_inner, "tensor", split_axis=0, concat_axis=1, tiled=True)
+    arrived = jnp.concatenate(
+        lax.all_to_all(
+            jnp.stack(jnp.split(up_inner, lax.axis_size("tensor"), axis=0)), "tensor", 0, 0
+        ),
+        axis=1,
+    )
     mixed_piece = arrived.reshape(hid_blocks, block_width, arrived.shape[3])
     pre_piece = jnp.einsum("jbt,jbc->jct", mixed_piece, first_left, preferred_element_type=fp)
     hidden = gelu_value(pre_piece).astype(bf)

time: 505 us -> 523 us (1.036)
  local copies, waits for them, and re-layouts: 19.5 us -> 37.7 us
    unnamed x23 -> x54, local copies, waits for them, and re-layouts: 8.76 us -> 27.9 us
where the time goes in v1:
time: 523 us; the launch traced here: 522 us
  waiting for transfers between devices  407 us (78%)
  local copies, waits for them, and re-layouts  37.7 us (7%)
  starting transfers between devices  37.7 us (7%)
  matrix products  20.8 us (4%)
  between operations  14.6 us (3%)
    unnamed x4, waiting for transfers between devices  192 us
    reduce_scatter x1, waiting for transfers between devices, shards(): lax.psum_scatter((jnp.einsum('kwt,tkc->wkc', mixed_down, cot_parts, prefe...  76.8 us
    reduce_scatter x1, waiting for transfers between devices, shards(): lax.psum_scatter((result.reshape(block_width, hid_blocks, block_width) *...  73.9 us
    unnamed x54, local copies, waits for them, and re-layouts  27.9 us
    all_to_all x1, waiting for transfers between devices, shards(): lax.all_to_all(jnp.stack(jnp.split(up_inner, lax.axis_size('tensor'), axi...  24.4 us
    all_to_all x1, waiting for transfers between devices, shards(): lax.all_to_all(down_inner, 'tensor', split_axis=0, concat_axis=1, tiled=T...  20.4 us
    all_to_all x1, waiting for transfers between devices, shards(): lax.all_to_all(d_mixed_down, 'tensor', split_axis=1, concat_axis=0, tiled...  19.5 us
    all_to_all x1, starting transfers between devices, shards(): lax.all_to_all(jnp.stack(jnp.split(up_inner, lax.axis_size('tensor'), axi...  14.3 us
  transfers between devices with their start and end apart: 7, of which 6 were waited for; matrix products, arithmetic and copies ran while one was open for 7% of the time, Pallas kernels for 0%

profile of v1, /device:TPU:1, one launch (start us, length us, event | category | flops | bytes accessed | tf_op | source)
XLA Modules:
  0.0 521.9 jit_solution(12103484247657466501)
XLA Ops:
  7.2 1.3 copy.49
  8.5 1.4 convolution_convert_fusion.1
  9.9 0.6 constant_dynamic-update-slice_fusion.31
  10.6 0.6 constant_dynamic-update-slice_fusion.30
  14.3 0.6 constant_dynamic-update-slice_fusion.24
  15.5 0.6 constant_dynamic-update-slice_fusion.22
  16.8 0.6 constant_dynamic-update-slice_fusion.20
  20.4 0.6 constant_dynamic-update-slice_fusion.14
  22.3 0.6 constant_dynamic-update-slice_fusion.11
  22.9 0.6 constant_dynamic-update-slice_fusion.10
  24.2 0.6 constant_dynamic-update-slice_fusion.8
  25.4 0.6 constant_dynamic-update-slice_fusion.6
  26.7 0.6 constant_dynamic-update-slice_fusion.4
  27.9 0.6 constant_dynamic-update-slice_fusion.2
  29.8 14.3 %all-to-all-start = ((bf16[32,4,1,8,512]{4,1,3,2,0:T(4,128)(2,1)}), bf16[32,4,1,8,512]{4,1,3,2,0:T(4,128)(2,1)S(1)}, u32[]{:S(2)}, u32[]{:S(2)}) async-start(bf16[32,4,1,8,512]{4,1,3,2,0:T(4,128)(2,1)} %constant_dynamic-update-slice_fusion), calls=%async_computation | async-start | bytes 2097152 | tf_op jit(solution)/shard_map/all_to_all | solution.py:43
  44.1 1.5 fusion.10
  45.5 24.4 %all-to-all-done = bf16[32,4,1,8,512]{4,1,3,2,0:T(4,128)(2,1)S(1)} async-done(((bf16[32,4,1,8,512]{4,1,3,2,0:T(4,128)(2,1)}), bf16[32,4,1,8,512]{4,1,3,2,0:T(4,128)(2,1)S(1)}, u32[]{:S(2)}, u32[]{:S(2)}) %all-to-all-start) | async-done | bytes 1048608 | tf_op jit(solution)/shard_map/all_to_all | solution.py:43
  69.9 7.5 %all-to-all-start.2 = ((bf16[1,128,8,512]{3,2,0,1:T(8,128)(2,1)}), bf16[1,128,8,512]{3,2,0,1:T(8,128)(2,1)S(1)}, u32[]{:S(2)}, u32[]{:S(2)}) async-start(bf16[1,128,8,512]{3,2,0,1:T(8,128)(2,1)} %fusion.10), calls=%async_computation.2 | async-start | bytes 2097152 | tf_op jit(solution)/shard_map/all_to_all | solution.py:65
  77.5 2.0 copy.52
  80.1 1.3 copy-done.1
  81.4 0.7 fusion.11
  82.1 1.5 copy.55
  83.7 19.5 %all-to-all-done.2 = bf16[1,128,8,512]{3,2,0,1:T(8,128)(2,1)S(1)} async-done(((bf16[1,128,8,512]{3,2,0,1:T(8,128)(2,1)}), bf16[1,128,8,512]{3,2,0,1:T(8,128)(2,1)S(1)}, u32[]{:S(2)}, u32[]{:S(2)}) %all-to-all-start.2) | async-done | bytes 1048608 | tf_op jit(solution)/shard_map/all_to_all | solution.py:65
  103.2 1.0 copy-done.3
  104.2 7.7 %all-to-all-start.1 = ((bf16[32,4,8,512]{3,2,1,0:T(8,128)(2,1)}), bf16[32,4,8,512]{3,2,1,0:T(8,128)(2,1)S(1)}, u32[]{:S(2)}, u32[]{:S(2)}) async-start(bf16[32,4,8,512]{3,2,1,0:T(8,128)(2,1)} %copy.55), calls=%async_computation.1 | async-start | bytes 2097152 | tf_op jit(solution)/shard_map/all_to_all | solution.py:54
  111.9 3.2 fusion.5
  116.1 1.1 copy.59
  117.2 20.4 %all-to-all-done.1 = bf16[32,4,8,512]{3,2,1,0:T(8,128)(2,1)S(1)} async-done(((bf16[32,4,8,512]{3,2,1,0:T(8,128)(2,1)}), bf16[32,4,8,512]{3,2,1,0:T(8,128)(2,1)S(1)}, u32[]{:S(2)}, u32[]{:S(2)}) %all-to-all-start.1) | async-done | bytes 1048608 | tf_op jit(solution)/shard_map/all_to_all | solution.py:54
  137.6 7.9 %all-to-all-start.3 = ((bf16[4,32,8,512]{3,2,0,1:T(8,128)(2,1)}), bf16[4,32,8,512]{3,2,0,1:T(8,128)(2,1)}, u32[]{:S(2)}, u32[]{:S(2)}) async-start(bf16[4,32,8,512]{3,2,0,1:T(8,128)(2,1)} %copy.59), calls=%async_computation.3 | async-start | bytes 2097152 | tf_op jit(solution)/shard_map/all_to_all | solution.py:70
  145.5 3.4 fusion.19
  148.9 2.0 copy.68
  151.0 1.3 dynamic-slice
  153.0 1.3 fusion.17
  154.5 2.6 fusion.20
  157.1 2.1 copy.65
  159.2 73.9 %reduce-scatter.3.cloned.1.call-done = bf16[16,4,256]{2,0,1:T(8,128)(2,1)} async-done(((bf16[256,4,256]{2,0,1:T(8,128)(2,1)}), bf16[16,4,256]{2,0,1:T(8,128)(2,1)}) %reduce-scatter.3.cloned.1.call-update) | async-done | bytes 32784 | tf_op jit(solution)/shard_map/reduce_scatter | solution.py:95
  233.1 1.4 convert_bitcast_fusion
  234.5 2.0 fusion.18
  236.8 2.1 copy.62
  238.9 1.2 convolution_convert_fusion.4
  240.1 2.5 fusion.21
  242.6 76.8 %reduce-scatter.5.cloned.1.call-done = bf16[64,1,256]{2,0,1:T(8,128)(2,1)} async-done(((bf16[1024,1,256]{2,0,1:T(8,128)(2,1)}), bf16[64,1,256]{2,0,1:T(8,128)(2,1)}) %reduce-scatter.5.cloned.1.call-update) | async-done | bytes 32784 | tf_op jit(solution)/shard_map/reduce_scatter | solution.py:103
  319.4 1.4 bitcast_convert_fusion.1
  320.8 191.6 %all-reduce.5.cloned.1.call-done = (bf16[256,1,1024]{2,1,0:T(2,128)(2,1)}, bf16[256,4,256]{2,1,0:T(4,128)(2,1)}) async-done(((bf16[256,1,1024]{2,1,0:T(2,128)(2,1)}, bf16[256,4,256]{2,1,0:T(4,128)(2,1)}), (bf16[256,1,1024]{2,1,0:T(2,128)(2,1)}, bf16[256,4,256]{2,1,0:T(4,128)(2,1)})) %all-reduce.5.cloned.1.call-update) | async-done | bytes 1048592
  512.4 0.9 bitcast_convert_fusion
  513.3 0.8 convert_bitcast_fusion.1
  514.1 0.6 copy.70
  514.7 0.6 copy.69
  (46 shorter events, 14.5 us)
Async XLA Ops:
  7.2 72.4 %copy-start = (bf16[4,256,256]{2,1,0:T(8,128)(2,1)S(1)}, bf16[4,256,256]{2,1,0:T(8,128)(2,1)}, u32[]{:S(2)}) copy-start(bf16[4,256,256]{2,1,0:T(8,128)(2,1)} %param.8) | copy-start | bytes 1572868
  9.9 34.1 %copy-start.4 = (bf16[1,1024,256]{2,1,0:T(8,128)(2,1)S(1)}, bf16[1,1024,256]{2,1,0:T(8,128)(2,1)}, u32[]{:S(2)}) copy-start(bf16[1,1024,256]{2,1,0:T(8,128)(2,1)} %param.10) | copy-start | bytes 1572868
  9.9 34.1 %copy-start.7 = (bf16[512,256]{1,0:T(8,128)(2,1)S(1)}, bf16[512,256]{1,0:T(8,128)(2,1)}, u32[]{:S(2)}) copy-start(bf16[512,256]{1,0:T(8,128)(2,1)} %param.11) | copy-start | bytes 786436
  29.8 40.2 %all-to-all-start = ((bf16[32,4,1,8,512]{4,1,3,2,0:T(4,128)(2,1)}), bf16[32,4,1,8,512]{4,1,3,2,0:T(4,128)(2,1)S(1)}, u32[]{:S(2)}, u32[]{:S(2)}) async-start(bf16[32,4,1,8,512]{4,1,3,2,0:T(4,128)(2,1)} %constant_dynamic-update-slice_fusion), calls=%async_computation | async-start | bytes 2097152 | tf_op jit(solution)/shard_map/all_to_all | solution.py:43
  69.9 33.2 %all-to-all-start.2 = ((bf16[1,128,8,512]{3,2,0,1:T(8,128)(2,1)}), bf16[1,128,8,512]{3,2,0,1:T(8,128)(2,1)S(1)}, u32[]{:S(2)}, u32[]{:S(2)}) async-start(bf16[1,128,8,512]{3,2,0,1:T(8,128)(2,1)} %fusion.10), calls=%async_computation.2 | async-start | bytes 2097152 | tf_op jit(solution)/shard_map/all_to_all | solution.py:65
  79.5 1.9 copy-start.6
  80.1 1.3 copy-start.1
  103.2 1.0 copy-start.3
  104.2 33.4 %all-to-all-start.1 = ((bf16[32,4,8,512]{3,2,1,0:T(8,128)(2,1)}), bf16[32,4,8,512]{3,2,1,0:T(8,128)(2,1)S(1)}, u32[]{:S(2)}, u32[]{:S(2)}) async-start(bf16[32,4,8,512]{3,2,1,0:T(8,128)(2,1)} %copy.55), calls=%async_computation.1 | async-start | bytes 2097152 | tf_op jit(solution)/shard_map/all_to_all | solution.py:54
  115.1 1.0 copy-start.2
  137.6 96.8 %all-to-all-start.3 = ((bf16[4,32,8,512]{3,2,0,1:T(8,128)(2,1)}), bf16[4,32,8,512]{3,2,0,1:T(8,128)(2,1)}, u32[]{:S(2)}, u32[]{:S(2)}) async-start(bf16[4,32,8,512]{3,2,0,1:T(8,128)(2,1)} %copy.59), calls=%async_computation.3 | async-start | bytes 2097152 | tf_op jit(solution)/shard_map/all_to_all | solution.py:70
  145.5 87.6 %reduce-scatter.3.cloned.1.call-start = ((), (), s32[]{:S(2)}) async-start(), calls=%async_computation.6 | async-start | bytes 557056 | tf_op jit(solution)/shard_map/reduce_scatter | solution.py:95
  151.0 168.4 %reduce-scatter.5.cloned.1.call-start = ((), (), s32[]{:S(2)}) async-start(), calls=%async_computation.7 | async-start | bytes 557056 | tf_op jit(solution)/shard_map/reduce_scatter | solution.py:103
  154.3 80.2 %copy-start.8 = (bf16[512,256]{1,0:T(8,128)(2,1)S(1)}, bf16[512,256]{1,0:T(8,128)(2,1)}, u32[]{:S(2)}) copy-start(bf16[512,256]{1,0:T(8,128)(2,1)} %param.6) | copy-start | bytes 786436
  154.3 358.1 %all-reduce.5.cloned.1.call-start = ((), (), s32[]{:S(2)}) async-start(), calls=%async_computation.8 | async-start | bytes 3145728
  234.5 4.5 copy-start.5
Sparse Core Ops, SparseCore 0:
  151.1 81.9 reduce-scatter.2
  237.7 81.6 reduce-scatter.4
  322.4 189.9 all-reduce.4
